TPU v7x, 32 devices: a whole 2x2x4 slice. The times are simulated.
32 devices in a mesh: sky: 8 (over z, y), los: 4 (over x, core).
Axes of the slice: x: 2, y: 2, z: 4, core: 2. Of those that a mesh axis runs over, the one named last changes fastest.
Arguments:
- features: bfloat16 [32, 16, 32, 128], P(None, 'sky', 'los'), may hold values from -6 to 6
- pre_first: bfloat16 [32, 16, 32, 128], P(None, 'sky', 'los'), may hold values from -8 to 8
- pre_second: bfloat16 [32, 16, 32, 128], P(None, 'sky', 'los'), may hold values from -8 to 8
- w_first: bfloat16 [3, 3, 3, 32, 32], replicated, may hold values from -0.21875 to 0.21875
- w_second: bfloat16 [3, 3, 3, 32, 32], replicated, may hold values from -0.21875 to 0.21875
- w_out: bfloat16 [3, 32], replicated, may hold values from -1 to 1
- b_out: float32 [3], replicated, may hold values from -1 to 1
- y_target: float32 [16, 128], P('sky'), may hold values from -6 to 6
- k_target: float32 [16, 128], P('sky'), may hold values from -6 to 6
Outputs:
- grad_features: bfloat16 [32, 16, 32, 128], P(None, 'sky', 'los')
- grad_first: float32 [3, 3, 3, 32, 32], replicated
- grad_second: float32 [3, 3, 3, 32, 32], replicated
- grad_out: float32 [3, 32], replicated
- grad_bias: float32 [3], replicated
All inputs are finite; a program needn't handle non-finite values.
Results may differ from a plain program's by a relative error of at most 0.0067.
Values may be sent and summed in bfloat16 or wider, within the bound.
No kernel may reach another device: no remote copies, remote signals or barrier semaphores. Data moves between devices by JAX's collectives and lax.ppermute only.
A program may use at most 64 MiB of HBM per device.

v0:
```python
import math
import jax
import jax.numpy as jnp
from jax import lax
from jax.sharding import PartitionSpec as P


def extended(block, sides, width):
    for axis, dim in sides:
        count = lax.axis_size(axis)
        forward = [(i, i + 1) for i in range(count - 1)]
        forward.append((count - 1, 0))
        backward = [(target, source) for source, target in forward]
        low = lax.ppermute(
            lax.slice_in_dim(block, block.shape[dim] - width, None, axis=dim), axis, forward
        )
        high = lax.ppermute(lax.slice_in_dim(block, 0, width, axis=dim), axis, backward)
        block = jnp.concatenate([low, block, high], axis=dim)
    return block


def silu_slope(value):
    sigma = jax.nn.sigmoid(value)
    return sigma * (1.0 + value * (1.0 - sigma))


def wrap_columns(field):
    return jnp.concatenate((field[..., -1:], field, field[..., :1]), axis=-1)


def spread_local(weight, padded, shape):
    result = jnp.zeros(shape, jnp.float32)
    for tap_x in range(3):
        for tap_z in range(3):
            for tap_y in range(3):
                window = padded[
                    :,
                    2 - tap_x : 2 - tap_x + shape[1],
                    2 - tap_z : 2 - tap_z + shape[2],
                    2 - tap_y : 2 - tap_y + shape[3],
                ]
                result = result + jnp.einsum(
                    "oi,oxzy->ixzy",
                    weight[tap_x, tap_z, tap_y],
                    window,
                    preferred_element_type=jnp.float32,
                )
    return result


def taps_from_inputs(grad_field, padded_inputs):
    shape = grad_field.shape
    taps_list = []
    for tap_x in range(3):
        for tap_z in range(3):
            for tap_y in range(3):
                window = padded_inputs[
                    :, tap_x : tap_x + shape[1], tap_z : tap_z + shape[2], tap_y : tap_y + shape[3]
                ]
                taps_list.append(
                    jnp.einsum(
                        "oxzy,ixzy->oi", grad_field, window, preferred_element_type=jnp.float32
                    )
                )
    return jnp.stack(taps_list).reshape(3, 3, 3, shape[0], padded_inputs.shape[0])


def per_device(
    features, pre_first, pre_second, w_first, w_second, w_out, b_out, y_target, k_target
):
    count_sky = lax.axis_size("sky")
    count_los = lax.axis_size("los")
    depth_all = pre_first.shape[2] * count_los
    norm_factor = 1.0 / math.sqrt(features.shape[1] * count_sky * features.shape[3] * depth_all)
    shape = features.shape
    first_wide = pre_first.astype(jnp.float32)
    second_wide = pre_second.astype(jnp.float32)
    hidden_second = jax.nn.silu(second_wide).astype(jnp.bfloat16)
    heads_raw = jnp.einsum(
        "oi,ixzy->oxzy", w_out, hidden_second, preferred_element_type=jnp.float32
    )
    heads_raw = heads_raw + b_out[:, None, None, None]
    pressure = jax.nn.softplus(heads_raw[0])
    density = jax.nn.softplus(heads_raw[1])
    velocity = heads_raw[2]
    y_part = jnp.sum(pressure, axis=1) / depth_all
    k_part = -jnp.sum(density * velocity, axis=1) / depth_all
    y_map, k_map = lax.psum((y_part, k_part), "los")
    y_resid = y_map - y_target
    k_resid = k_map - k_target
    y_resid = y_resid[:, None, :]
    k_resid = k_resid[:, None, :]
    head_grad = jnp.stack(
        (
            y_resid * jax.nn.sigmoid(heads_raw[0]),
            -k_resid * velocity * jax.nn.sigmoid(heads_raw[1]),
            -k_resid * density,
        )
    ).astype(jnp.bfloat16)
    grad_out = (
        jnp.einsum("oxzy,ixzy->oi", head_grad, hidden_second, preferred_element_type=jnp.float32)
        * norm_factor
    )
    grad_bias = jnp.sum(head_grad.astype(jnp.float32), axis=(1, 2, 3)) * norm_factor
    back_second = jnp.einsum("oi,oxzy->ixzy", w_out, head_grad, preferred_element_type=jnp.float32)
    grad_second_pre = (back_second * silu_slope(second_wide)).astype(jnp.bfloat16)
    second_padded = wrap_columns(extended(grad_second_pre, (("sky", 1), ("los", 2)), 1))
    back_first = spread_local(w_second, second_padded, shape)
    grad_first_pre = (back_first * silu_slope(first_wide)).astype(jnp.bfloat16)
    first_padded = wrap_columns(extended(grad_first_pre, (("sky", 1), ("los", 2)), 1))
    grad_features = spread_local(w_first, first_padded, shape).astype(jnp.bfloat16)
    saved_padded = wrap_columns(
        extended(jnp.stack((features, pre_first)), (("sky", 2), ("los", 3)), 1)
    )
    hidden_padded = jax.nn.silu(saved_padded[1].astype(jnp.float32)).astype(jnp.bfloat16)
    grad_second = taps_from_inputs(grad_second_pre, hidden_padded)
    grad_first = taps_from_inputs(grad_first_pre, saved_padded[0])
    grad_first, grad_second, grad_out, grad_bias = lax.psum(
        (grad_first * norm_factor, grad_second * norm_factor, grad_out, grad_bias), ("sky", "los")
    )
    return (grad_features, grad_first, grad_second, grad_out, grad_bias)


def solution(mesh):
    in_specs = (
        P(None, "sky", "los", None),
        P(None, "sky", "los", None),
        P(None, "sky", "los", None),
        P(),
        P(),
        P(),
        P(),
        P("sky", None),
        P("sky", None),
    )
    out_specs = (P(None, "sky", "los", None), P(), P(), P(), P())
    return jax.shard_map(
        per_device, mesh=mesh, in_specs=in_specs, out_specs=out_specs, check_vma=False
    )
```

profile of v0, /device:TPU:0, one launch (start us, length us, event | category | flops | bytes accessed | tf_op | source)
XLA Modules:
  0.0 245.4 jit_solution(12712252060760157756)
XLA Ops:
  7.3 1.0 copy.311
  8.2 0.9 copy.312
  9.2 3.0 %collective-permute-start.8 = (bf16[2,32,1,8,128]{4,1,3,2,0:T(8,128)(2,1)S(1)}, bf16[2,32,1,8,128]{4,1,3,2,0:T(8,128)(2,1)S(1)}, u32[]{:S(2)}, u32[]{:S(2)}) collective-permute-start(bf16[2,32,1,8,128]{4,1,3,2,0:T(8,128)(2,1)S(1)} %get-tuple-element.37), channel_id=1, source_target_pairs={{0,4},{4,8},{8,12},{12,16},{16,20},{20,24},{24,28},{28,0},{1,5},{5... | collective-permute-start | bytes 393224 | tf_op jit(solution)/shard_map/ppermute | solution.py:14
  12.2 3.1 %collective-permute-start.9 = (bf16[2,32,1,8,128]{4,1,3,2,0:T(8,128)(2,1)S(1)}, bf16[2,32,1,8,128]{4,1,3,2,0:T(8,128)(2,1)S(1)}, u32[]{:S(2)}, u32[]{:S(2)}) collective-permute-start(bf16[2,32,1,8,128]{4,1,3,2,0:T(8,128)(2,1)S(1)} %get-tuple-element.38), channel_id=1, source_target_pairs={{4,0},{8,4},{12,8},{16,12},{20,16},{24,20},{28,24},{0,28},{5,1},{9... | collective-permute-start | bytes 393224 | tf_op jit(solution)/shard_map/ppermute | solution.py:17
  15.3 1.0 fusion.100
  16.6 6.3 %all-reduce.2 = (f32[2,128]{1,0:T(2,128)S(1)}, f32[2,128]{1,0:T(2,128)S(1)}) all-reduce(f32[2,128]{1,0:T(2,128)S(1)} %get-tuple-element.54, f32[2,128]{1,0:T(2,128)S(1)} %get-tuple-element.55), channel_id=1, replica_groups=mesh['sky'=8,'los'=4] {'los'}, use_global_device_ids=true, to_apply=%region_3.4 | all-reduce | flops 512 | bytes 4096 | tf_op jit(solution)/shard_map/psum | solution.py:88
  23.4 4.7 %collective-permute-start.1 = (bf16[32,1,8,128]{3,0,2,1:T(8,128)(2,1)S(1)}, bf16[32,1,8,128]{3,0,2,1:T(8,128)(2,1)S(1)}, u32[]{:S(2)}, u32[]{:S(2)}) collective-permute-start(bf16[32,1,8,128]{3,0,2,1:T(8,128)(2,1)S(1)} %get-tuple-element.50), channel_id=1, source_target_pairs={{4,0},{8,4},{12,8},{16,12},{20,16},{24,20},{28,24},{0,28},{5,1},{9... | collective-permute-start | bytes 196616 | tf_op jit(solution)/shard_map/ppermute | solution.py:17
  28.2 2.1 collective-permute-done
  30.4 1.7 collective-permute-start.3
  32.2 39.6 %all-reduce = (f32[3,32]{1,0:T(4,128)}, f32[3]{0:T(128)}) all-reduce(f32[3,32]{1,0:T(4,128)S(1)} %fusion.91, f32[3]{0:T(128)S(1)} %broadcast_multiply_fusion.3), channel_id=1, replica_groups=mesh['sky'=8,'los'=4] {'sky','los'}, use_global_device_ids=true, to_apply=%region_6.7 | all-reduce | flops 99 | bytes 792 | tf_op jit(solution)/shard_map/psum | solution.py:118
  72.0 0.5 pad_maximum_fusion.1
  72.5 0.4 copy-done.2
  75.2 0.2 convolution_add_fusion.25
  75.7 0.2 convolution_add_fusion.23
  76.2 0.2 convolution_add_fusion.21
  76.6 0.2 convolution_add_fusion.19
  77.1 0.2 convolution_add_fusion.17
  77.8 0.2 convolution_add_fusion.14
  78.0 0.2 fusion.32
  78.5 0.2 fusion.26
  79.4 2.6 %collective-permute-start.4 = (bf16[32,1,8,128]{3,0,2,1:T(8,128)(2,1)S(1)}, bf16[32,1,8,128]{3,0,2,1:T(8,128)(2,1)S(1)}, u32[]{:S(2)}, u32[]{:S(2)}) collective-permute-start(bf16[32,1,8,128]{3,0,2,1:T(8,128)(2,1)S(1)} %get-tuple-element.47), channel_id=1, source_target_pairs={{0,4},{4,8},{8,12},{12,16},{16,20},{20,24},{24,28},{28,0},{1,5},{5... | collective-permute-start | bytes 196616 | tf_op jit(solution)/shard_map/ppermute | solution.py:14
  82.0 2.2 collective-permute-start.5
  84.3 1.7 collective-permute-start.11
  86.0 0.5 collective-permute-done.4
  86.6 0.4 collective-permute-done.5
  87.1 1.7 collective-permute-start.7
  88.9 0.3 fusion.349
  89.2 0.8 pad_maximum_fusion
  90.0 0.4 fusion.3
  90.6 0.2 fusion.62
  91.3 0.2 fusion.59
  91.9 0.2 fusion.56
  92.6 0.2 fusion.53
  93.3 0.2 fusion.50
  93.9 0.2 fusion.47
  94.6 0.2 fusion.44
  95.2 0.3 fusion.41
  95.9 0.2 fusion.38
  96.2 0.2 fusion.37
  96.4 0.8 broadcast_multiply_fusion
  97.4 0.2 fusion.89
  98.0 0.2 fusion.86
  98.7 0.2 fusion.83
  99.4 0.2 fusion.80
  100.0 0.2 fusion.77
  100.7 0.3 fusion.74
  101.3 0.2 fusion.71
  102.0 0.2 fusion.68
  102.7 0.2 fusion.65
  103.2 0.8 broadcast_multiply_fusion.1
  104.3 0.5 pad_maximum_fusion.2
  104.8 0.4 copy-done.1
  107.5 0.2 convolution_add_fusion.12
  107.9 0.2 convolution_add_fusion.10
  108.4 0.2 convolution_add_fusion.8
  108.9 0.2 convolution_add_fusion.6
  109.3 0.2 convolution_add_fusion.4
  110.0 0.2 convolution_add_fusion.1
  110.3 0.2 fusion.30
  110.8 0.2 fusion.20
  111.4 0.7 copy.134
  112.1 122.8 %all-reduce.5.cloned.1.call-done = (f32[3,3,3,32,32]{4,3,2,1,0:T(8,128)}, f32[3,3,3,32,32]{4,3,2,1,0:T(8,128)}) async-done(((f32[3,3,3,32,32]{4,3,2,1,0:T(8,128)}, f32[3,3,3,32,32]{4,3,2,1,0:T(8,128)}), (f32[3,3,3,32,32]{4,3,2,1,0:T(8,128)}, f32[3,3,3,32,32]{4,3,2,1,0:T(8,128)})) %all-reduce.5.cloned.1.call-update) | async-done | bytes 221200 | tf_op jit(solution)/shard_map/psum | solution.py:118
  235.0 1.8 copy.367
  236.8 1.8 copy.368
  (127 shorter events, 17.3 us)
Async XLA Ops:
  7.2 9.2 %copy-start = (bf16[3,32]{1,0:T(4,128)(2,1)S(1)}, bf16[3,32]{1,0:T(4,128)(2,1)}, u32[]{:S(2)}) copy-start(bf16[3,32]{1,0:T(4,128)(2,1)} %param.14) | copy-start | bytes 580
  7.2 15.9 %copy-start.3 = (bf16[32,2,8,128]{3,2,1,0:T(8,128)(2,1)S(1)}, bf16[32,2,8,128]{3,2,1,0:T(8,128)(2,1)}, u32[]{:S(2)}) copy-start(bf16[32,2,8,128]{3,2,1,0:T(8,128)(2,1)} %param.11) | copy-start | bytes 393220
  7.2 9.3 %copy-start.7 = (f32[3]{0:T(128)S(1)}, f32[3]{0:T(128)}, u32[]{:S(2)}) copy-start(f32[3]{0:T(128)} %param.15) | copy-start | bytes 40
  7.2 15.7 %copy-start.5 = (f32[2,128]{1,0:T(2,128)S(1)}, f32[2,128]{1,0:T(2,128)}, u32[]{:S(2)}) copy-start(f32[2,128]{1,0:T(2,128)} %param.16) | copy-start | bytes 3076
  7.2 15.7 %copy-start.6 = (f32[2,128]{1,0:T(2,128)S(1)}, f32[2,128]{1,0:T(2,128)}, u32[]{:S(2)}) copy-start(f32[2,128]{1,0:T(2,128)} %param.17) | copy-start | bytes 3076
  7.2 227.8 %all-reduce.5.cloned.1.call-start = ((), (), s32[]{:S(2)}) async-start(), calls=%async_computation | async-start | bytes 1769472 | tf_op jit(solution)/shard_map/psum | solution.py:118
  9.2 75.0 %collective-permute-start.8 = (bf16[2,32,1,8,128]{4,1,3,2,0:T(8,128)(2,1)S(1)}, bf16[2,32,1,8,128]{4,1,3,2,0:T(8,128)(2,1)S(1)}, u32[]{:S(2)}, u32[]{:S(2)}) collective-permute-start(bf16[2,32,1,8,128]{4,1,3,2,0:T(8,128)(2,1)S(1)} %get-tuple-element.37), channel_id=1, source_target_pairs={{0,4},{4,8},{8,12},{12,16},{16,20},{20,24},{24,28},{28,0},{1,5},{5... | collective-permute-start | bytes 393224 | tf_op jit(solution)/shard_map/ppermute | solution.py:14
  12.2 72.0 %collective-permute-start.9 = (bf16[2,32,1,8,128]{4,1,3,2,0:T(8,128)(2,1)S(1)}, bf16[2,32,1,8,128]{4,1,3,2,0:T(8,128)(2,1)S(1)}, u32[]{:S(2)}, u32[]{:S(2)}) collective-permute-start(bf16[2,32,1,8,128]{4,1,3,2,0:T(8,128)(2,1)S(1)} %get-tuple-element.38), channel_id=1, source_target_pairs={{4,0},{8,4},{12,8},{16,12},{20,16},{24,20},{28,24},{0,28},{5,1},{9... | collective-permute-start | bytes 393224 | tf_op jit(solution)/shard_map/ppermute | solution.py:17
  23.3 7.0 %collective-permute-start = (bf16[32,1,8,128]{3,0,2,1:T(8,128)(2,1)S(1)}, bf16[32,1,8,128]{3,0,2,1:T(8,128)(2,1)S(1)}, u32[]{:S(2)}, u32[]{:S(2)}) collective-permute-start(bf16[32,1,8,128]{3,0,2,1:T(8,128)(2,1)S(1)} %get-tuple-element.49), channel_id=1, source_target_pairs={{0,4},{4,8},{8,12},{12,16},{16,20},{20,24},{24,28},{28,0},{1,5},{5... | collective-permute-start | bytes 196616 | tf_op jit(solution)/shard_map/ppermute | solution.py:14
  23.4 7.0 %collective-permute-start.1 = (bf16[32,1,8,128]{3,0,2,1:T(8,128)(2,1)S(1)}, bf16[32,1,8,128]{3,0,2,1:T(8,128)(2,1)S(1)}, u32[]{:S(2)}, u32[]{:S(2)}) collective-permute-start(bf16[32,1,8,128]{3,0,2,1:T(8,128)(2,1)S(1)} %get-tuple-element.50), channel_id=1, source_target_pairs={{4,0},{8,4},{12,8},{16,12},{20,16},{24,20},{28,24},{0,28},{5,1},{9... | collective-permute-start | bytes 196616 | tf_op jit(solution)/shard_map/ppermute | solution.py:17
  30.4 41.4 %collective-permute-start.2 = (bf16[32,4,1,128]{3,0,2,1:T(8,128)(2,1)S(1)}, bf16[32,4,1,128]{3,0,2,1:T(8,128)(2,1)S(1)}, u32[]{:S(2)}, u32[]{:S(2)}) collective-permute-start(bf16[32,4,1,128]{3,0,2,1:T(8,128)(2,1)S(1)} %get-tuple-element.45), channel_id=1, source_target_pairs={{0,1},{1,2},{2,3},{3,0},{4,5},{5,6},{6,7},{7,4},{8,9},{9,10},{10,1... | collective-permute-start | bytes 98312 | tf_op jit(solution)/shard_map/ppermute | solution.py:14
  30.4 41.4 %collective-permute-start.3 = (bf16[32,4,1,128]{3,0,2,1:T(8,128)(2,1)S(1)}, bf16[32,4,1,128]{3,0,2,1:T(8,128)(2,1)S(1)}, u32[]{:S(2)}, u32[]{:S(2)}) collective-permute-start(bf16[32,4,1,128]{3,0,2,1:T(8,128)(2,1)S(1)} %get-tuple-element.46), channel_id=1, source_target_pairs={{1,0},{2,1},{3,2},{0,3},{5,4},{6,5},{7,6},{4,7},{9,8},{10,9},{11,1... | collective-permute-start | bytes 98312 | tf_op jit(solution)/shard_map/ppermute | solution.py:17
  72.0 0.9 copy-start.2
  78.3 0.9 copy-start.4
  79.4 7.1 %collective-permute-start.4 = (bf16[32,1,8,128]{3,0,2,1:T(8,128)(2,1)S(1)}, bf16[32,1,8,128]{3,0,2,1:T(8,128)(2,1)S(1)}, u32[]{:S(2)}, u32[]{:S(2)}) collective-permute-start(bf16[32,1,8,128]{3,0,2,1:T(8,128)(2,1)S(1)} %get-tuple-element.47), channel_id=1, source_target_pairs={{0,4},{4,8},{8,12},{12,16},{16,20},{20,24},{24,28},{28,0},{1,5},{5... | collective-permute-start | bytes 196616 | tf_op jit(solution)/shard_map/ppermute | solution.py:14
  82.0 5.0 %collective-permute-start.5 = (bf16[32,1,8,128]{3,0,2,1:T(8,128)(2,1)S(1)}, bf16[32,1,8,128]{3,0,2,1:T(8,128)(2,1)S(1)}, u32[]{:S(2)}, u32[]{:S(2)}) collective-permute-start(bf16[32,1,8,128]{3,0,2,1:T(8,128)(2,1)S(1)} %get-tuple-element.48), channel_id=1, source_target_pairs={{4,0},{8,4},{12,8},{16,12},{20,16},{24,20},{28,24},{0,28},{5,1},{9... | collective-permute-start | bytes 196616 | tf_op jit(solution)/shard_map/ppermute | solution.py:17
  84.2 4.6 %collective-permute-start.10 = (bf16[2,32,4,1,128]{4,1,3,2,0:T(8,128)(2,1)S(1)}, bf16[2,32,4,1,128]{4,1,3,2,0:T(8,128)(2,1)S(1)}, u32[]{:S(2)}, u32[]{:S(2)}) collective-permute-start(bf16[2,32,4,1,128]{4,1,3,2,0:T(8,128)(2,1)S(1)} %get-tuple-element.27), channel_id=1, source_target_pairs={{0,1},{1,2},{2,3},{3,0},{4,5},{5,6},{6,7},{7,4},{8,9},{9,10},{10,1... | collective-permute-start | bytes 196616 | tf_op jit(solution)/shard_map/ppermute | solution.py:14
  84.3 4.5 %collective-permute-start.11 = (bf16[2,32,4,1,128]{4,1,3,2,0:T(8,128)(2,1)S(1)}, bf16[2,32,4,1,128]{4,1,3,2,0:T(8,128)(2,1)S(1)}, u32[]{:S(2)}, u32[]{:S(2)}) collective-permute-start(bf16[2,32,4,1,128]{4,1,3,2,0:T(8,128)(2,1)S(1)} %get-tuple-element.28), channel_id=1, source_target_pairs={{1,0},{2,1},{3,2},{0,3},{5,4},{6,5},{7,6},{4,7},{9,8},{10,9},{11,1... | collective-permute-start | bytes 196616 | tf_op jit(solution)/shard_map/ppermute | solution.py:17
  87.0 17.0 %collective-permute-start.6 = (bf16[32,4,1,128]{3,0,2,1:T(8,128)(2,1)S(1)}, bf16[32,4,1,128]{3,0,2,1:T(8,128)(2,1)S(1)}, u32[]{:S(2)}, u32[]{:S(2)}) collective-permute-start(bf16[32,4,1,128]{3,0,2,1:T(8,128)(2,1)S(1)} %get-tuple-element.41), channel_id=1, source_target_pairs={{0,1},{1,2},{2,3},{3,0},{4,5},{5,6},{6,7},{7,4},{8,9},{9,10},{10,1... | collective-permute-start | bytes 98312 | tf_op jit(solution)/shard_map/ppermute | solution.py:14
  87.1 16.9 %collective-permute-start.7 = (bf16[32,4,1,128]{3,0,2,1:T(8,128)(2,1)S(1)}, bf16[32,4,1,128]{3,0,2,1:T(8,128)(2,1)S(1)}, u32[]{:S(2)}, u32[]{:S(2)}) collective-permute-start(bf16[32,4,1,128]{3,0,2,1:T(8,128)(2,1)S(1)} %get-tuple-element.42), channel_id=1, source_target_pairs={{1,0},{2,1},{3,2},{0,3},{5,4},{6,5},{7,6},{4,7},{9,8},{10,9},{11,1... | collective-permute-start | bytes 98312 | tf_op jit(solution)/shard_map/ppermute | solution.py:17
  104.3 0.9 copy-start.1
Sparse Core Ops, SparseCore 0:
  104.1 130.8 all-reduce.4
where the time goes:
time: 246 us; the launch traced here: 245 us
  waiting for transfers between devices  126 us (51%)
  blocking collectives  45.9 us (19%)
  matrix products  24.4 us (10%)
  starting transfers between devices  21.1 us (9%)
  between operations  14.7 us (6%)
  local copies, waits for them, and re-layouts  8.01 us (3%)
  other arithmetic  5.42 us (2%)
    psum x1, waiting for transfers between devices, per_device(): lax.psum((grad_first * norm_factor, grad_second * norm_factor, grad_out,...  123 us
    psum x1, blocking collectives, per_device(): lax.psum((grad_first * norm_factor, grad_second * norm_factor, grad_out,...  39.6 us
    ppermute x6, starting transfers between devices, extended(): lax.ppermute(lax.slice_in_dim(block, 0, width, axis=dim), axis, backward)  15.2 us
    dot_general x54, matrix products, spread_local(): jnp.einsum('oi,oxzy->ixzy', weight[tap_x, tap_z, tap_y], window, preferre...  12 us
    dot_general x54, matrix products, taps_from_inputs(): jnp.einsum('oxzy,ixzy->oi', grad_field, window, preferred_element_type=jn...  11.9 us
    unnamed x21, local copies, waits for them, and re-layouts  7.35 us
    psum x1, blocking collectives, per_device(): y_map, k_map = lax.psum((y_part, k_part), 'los')  6.31 us
    ppermute x6, starting transfers between devices, extended(): lax.ppermute(lax.slice_in_dim(block, block.shape[dim] - width, None, axis...  5.83 us
  transfers between devices with their start and end apart: 13, of which 4 were waited for; matrix products, arithmetic and copies ran while one was open for 13% of the time, Pallas kernels for 0%

commit v1 on v0

--- a/solution.py
+++ b/solution.py
@@ -115,8 +115,14 @@
     hidden_padded = jax.nn.silu(saved_padded[1].astype(jnp.float32)).astype(jnp.bfloat16)
     grad_second = taps_from_inputs(grad_second_pre, hidden_padded)
     grad_first = taps_from_inputs(grad_first_pre, saved_padded[0])
-    grad_first, grad_second, grad_out, grad_bias = lax.psum(
-        (grad_first * norm_factor, grad_second * norm_factor, grad_out, grad_bias), ("sky", "los")
+
+    def ends_scan(sample):
+        for kk in ("los", "sky"):
+            sample = lax.psum(sample, axis_name=kk)
+        return sample
+
+    grad_first, grad_second, grad_out, grad_bias = ends_scan(
+        (grad_first * norm_factor, grad_second * norm_factor, grad_out, grad_bias)
     )
     return (grad_features, grad_first, grad_second, grad_out, grad_bias)
 

time: 246 us -> 219 us (0.89)
  waiting for transfers between devices: 126 us -> 110 us
  blocking collectives: 45.9 us -> 34.3 us
    psum x1 -> x2, waiting for transfers between devices: 123 us -> 108 us  [ends_scan(): sample = lax.psum(sample, axis_name=kk)]
    psum x1 -> x2, blocking collectives: 39.6 us -> 28 us  [ends_scan(): sample = lax.psum(sample, axis_name=kk)]
    ppermute x6, starting transfers between devices: 5.83 us -> 3.31 us  [extended(): lax.ppermute(lax.slice_in_dim(block, block.shape[dim] - width, None, axis...]
    ppermute x6, starting transfers between devices: 15.2 us -> 17.7 us  [extended(): lax.ppermute(lax.slice_in_dim(block, 0, width, axis=dim), axis, backward)]
  transfers between devices with their start and end apart: 13 -> 14, of which waited for: 4 -> 4; matrix products, arithmetic and copies ran while one was open for 13% -> 14% of each run, Pallas kernels for 0% -> 0%
where the time goes in v1:
time: 219 us
  waiting for transfers between devices  110 us (50%)
  blocking collectives  34.3 us (16%)
  matrix products  24.4 us (11%)
  starting transfers between devices  21.3 us (10%)
  between operations  14.7 us (7%)
  local copies, waits for them, and re-layouts  8 us (4%)
  other arithmetic  5.42 us (2%)
    psum x2, waiting for transfers between devices, ends_scan(): sample = lax.psum(sample, axis_name=kk)  108 us
    psum x2, blocking collectives, ends_scan(): sample = lax.psum(sample, axis_name=kk)  28 us
    ppermute x6, starting transfers between devices, extended(): lax.ppermute(lax.slice_in_dim(block, 0, width, axis=dim), axis, backward)  17.7 us
    dot_general x54, matrix products, spread_local(): jnp.einsum('oi,oxzy->ixzy', weight[tap_x, tap_z, tap_y], window, preferre...  12 us
    dot_general x54, matrix products, taps_from_inputs(): jnp.einsum('oxzy,ixzy->oi', grad_field, window, preferred_element_type=jn...  11.9 us
    unnamed x21, local copies, waits for them, and re-layouts  7.35 us
    psum x1, blocking collectives, per_device(): y_map, k_map = lax.psum((y_part, k_part), 'los')  6.31 us
  transfers between devices with their start and end apart: 14, of which 4 were waited for; matrix products, arithmetic and copies ran while one was open for 14% of the time, Pallas kernels for 0%

profile of v1, /device:TPU:0, one launch (start us, length us, event | category | flops | bytes accessed | tf_op | source)
XLA Modules:
  0.0 218.5 jit_solution(4682568609867258302)
XLA Ops:
  7.3 1.0 copy.311
  8.2 0.9 copy.312
  9.2 3.0 %collective-permute-start.8 = (bf16[2,32,1,8,128]{4,1,3,2,0:T(8,128)(2,1)S(1)}, bf16[2,32,1,8,128]{4,1,3,2,0:T(8,128)(2,1)S(1)}, u32[]{:S(2)}, u32[]{:S(2)}) collective-permute-start(bf16[2,32,1,8,128]{4,1,3,2,0:T(8,128)(2,1)S(1)} %get-tuple-element.41), channel_id=1, source_target_pairs={{0,4},{4,8},{8,12},{12,16},{16,20},{20,24},{24,28},{28,0},{1,5},{5... | collective-permute-start | bytes 393224 | tf_op jit(solution)/shard_map/ppermute | solution.py:14
  12.2 3.1 %collective-permute-start.9 = (bf16[2,32,1,8,128]{4,1,3,2,0:T(8,128)(2,1)S(1)}, bf16[2,32,1,8,128]{4,1,3,2,0:T(8,128)(2,1)S(1)}, u32[]{:S(2)}, u32[]{:S(2)}) collective-permute-start(bf16[2,32,1,8,128]{4,1,3,2,0:T(8,128)(2,1)S(1)} %get-tuple-element.42), channel_id=1, source_target_pairs={{4,0},{8,4},{12,8},{16,12},{20,16},{24,20},{28,24},{0,28},{5,1},{9... | collective-permute-start | bytes 393224 | tf_op jit(solution)/shard_map/ppermute | solution.py:17
  15.3 1.0 fusion.100
  16.6 6.3 %all-reduce.3 = (f32[2,128]{1,0:T(2,128)S(1)}, f32[2,128]{1,0:T(2,128)S(1)}) all-reduce(f32[2,128]{1,0:T(2,128)S(1)} %get-tuple-element.58, f32[2,128]{1,0:T(2,128)S(1)} %get-tuple-element.59), channel_id=1, replica_groups=mesh['sky'=8,'los'=4] {'los'}, use_global_device_ids=true, to_apply=%region_3.4 | all-reduce | flops 512 | bytes 4096 | tf_op jit(solution)/shard_map/psum | solution.py:88
  23.4 4.7 %collective-permute-start.1 = (bf16[32,1,8,128]{3,0,2,1:T(8,128)(2,1)S(1)}, bf16[32,1,8,128]{3,0,2,1:T(8,128)(2,1)S(1)}, u32[]{:S(2)}, u32[]{:S(2)}) collective-permute-start(bf16[32,1,8,128]{3,0,2,1:T(8,128)(2,1)S(1)} %get-tuple-element.54), channel_id=1, source_target_pairs={{4,0},{8,4},{12,8},{16,12},{20,16},{24,20},{28,24},{0,28},{5,1},{9... | collective-permute-start | bytes 196616 | tf_op jit(solution)/shard_map/ppermute | solution.py:17
  28.2 2.1 collective-permute-done
  30.4 1.7 collective-permute-start.3
  32.2 5.6 %all-reduce.2 = (f32[3,32]{1,0:T(4,128)S(1)}, f32[3]{0:T(128)S(1)}) all-reduce(f32[3,32]{1,0:T(4,128)S(1)} %fusion.91, f32[3]{0:T(128)S(1)} %broadcast_multiply_fusion.3), channel_id=1, replica_groups=mesh['sky'=8,'los'=4] {'los'}, use_global_device_ids=true, to_apply=%region_8.9 | all-reduce | flops 99 | bytes 792 | tf_op jit(solution)/shard_map/psum | solution.py:121
  37.8 22.4 %all-reduce = (f32[3,32]{1,0:T(4,128)}, f32[3]{0:T(128)}) all-reduce(f32[3,32]{1,0:T(4,128)S(1)} %get-tuple-element.21, f32[3]{0:T(128)S(1)} %get-tuple-element.22), channel_id=1, replica_groups=mesh['sky'=8,'los'=4] {'sky'}, use_global_device_ids=true, to_apply=%region_9.10 | all-reduce | flops 99 | bytes 792 | tf_op jit(solution)/shard_map/psum | solution.py:121
  60.4 0.5 pad_maximum_fusion.1
  60.9 0.4 copy-done.2
  63.6 0.2 convolution_add_fusion.25
  64.1 0.2 convolution_add_fusion.23
  64.6 0.2 convolution_add_fusion.21
  65.0 0.2 convolution_add_fusion.19
  65.5 0.2 convolution_add_fusion.17
  66.2 0.2 convolution_add_fusion.14
  66.4 0.2 fusion.32
  66.9 0.2 fusion.26
  67.9 4.7 %collective-permute-start.5 = (bf16[32,1,8,128]{3,0,2,1:T(8,128)(2,1)S(1)}, bf16[32,1,8,128]{3,0,2,1:T(8,128)(2,1)S(1)}, u32[]{:S(2)}, u32[]{:S(2)}) collective-permute-start(bf16[32,1,8,128]{3,0,2,1:T(8,128)(2,1)S(1)} %get-tuple-element.52), channel_id=1, source_target_pairs={{4,0},{8,4},{12,8},{16,12},{20,16},{24,20},{28,24},{0,28},{5,1},{9... | collective-permute-start | bytes 196616 | tf_op jit(solution)/shard_map/ppermute | solution.py:17
  72.7 1.7 collective-permute-start.11
  74.4 0.4 collective-permute-done.4
  74.9 1.7 collective-permute-start.7
  76.8 0.3 fusion.349
  77.1 0.8 pad_maximum_fusion
  77.9 0.4 fusion.3
  78.5 0.2 fusion.62
  79.1 0.2 fusion.59
  79.8 0.3 fusion.56
  80.5 0.2 fusion.53
  80.7 0.2 fusion.52
  81.1 0.2 fusion.50
  81.8 0.2 fusion.47
  82.5 0.2 fusion.44
  83.1 0.2 fusion.41
  83.8 0.2 fusion.38
  84.3 0.8 broadcast_multiply_fusion
  85.2 0.2 fusion.89
  85.9 0.3 fusion.86
  86.6 0.2 fusion.83
  87.2 0.2 fusion.80
  87.5 0.3 fusion.79
  87.9 0.3 fusion.77
  89.2 0.3 fusion.71
  90.1 0.3 fusion.67
  90.6 0.2 fusion.65
  91.0 0.8 broadcast_multiply_fusion.1
  92.4 0.5 pad_maximum_fusion.2
  92.9 0.4 copy-done.1
  95.6 0.2 convolution_add_fusion.12
  96.0 0.2 convolution_add_fusion.10
  96.5 0.2 convolution_add_fusion.8
  97.0 0.2 convolution_add_fusion.6
  97.4 0.2 convolution_add_fusion.4
  98.1 0.2 convolution_add_fusion.1
  98.4 0.2 fusion.30
  98.9 0.2 fusion.20
  99.3 29.0 %all-reduce.10.cloned.1.call-done = (f32[3,3,3,32,32]{4,3,2,1,0:T(8,128)}, f32[3,3,3,32,32]{4,3,2,1,0:T(8,128)}) async-done(((f32[3,3,3,32,32]{4,3,2,1,0:T(8,128)}, f32[3,3,3,32,32]{4,3,2,1,0:T(8,128)}), (f32[3,3,3,32,32]{4,3,2,1,0:T(8,128)}, f32[3,3,3,32,32]{4,3,2,1,0:T(8,128)})) %all-reduce.10.cloned.1.call-update) | async-done | bytes 221200 | tf_op jit(solution)/shard_map/psum | solution.py:121
  128.5 0.7 copy.134
  129.2 78.9 %all-reduce.8.cloned.1.call-done = (f32[3,3,3,32,32]{4,3,2,1,0:T(8,128)}, f32[3,3,3,32,32]{4,3,2,1,0:T(8,128)}) async-done(((f32[3,3,3,32,32]{4,3,2,1,0:T(8,128)}, f32[3,3,3,32,32]{4,3,2,1,0:T(8,128)}), (f32[3,3,3,32,32]{4,3,2,1,0:T(8,128)}, f32[3,3,3,32,32]{4,3,2,1,0:T(8,128)})) %all-reduce.8.cloned.1.call-update) | async-done | bytes 221200 | tf_op jit(solution)/shard_map/psum | solution.py:121
  208.1 1.8 copy.369
  209.9 1.8 copy.370
  (131 shorter events, 17.5 us)
Async XLA Ops:
  7.2 9.2 %copy-start = (bf16[3,32]{1,0:T(4,128)(2,1)S(1)}, bf16[3,32]{1,0:T(4,128)(2,1)}, u32[]{:S(2)}) copy-start(bf16[3,32]{1,0:T(4,128)(2,1)} %param.14) | copy-start | bytes 580
  7.2 15.9 %copy-start.3 = (bf16[32,2,8,128]{3,2,1,0:T(8,128)(2,1)S(1)}, bf16[32,2,8,128]{3,2,1,0:T(8,128)(2,1)}, u32[]{:S(2)}) copy-start(bf16[32,2,8,128]{3,2,1,0:T(8,128)(2,1)} %param.11) | copy-start | bytes 393220
  7.2 9.3 %copy-start.7 = (f32[3]{0:T(128)S(1)}, f32[3]{0:T(128)}, u32[]{:S(2)}) copy-start(f32[3]{0:T(128)} %param.15) | copy-start | bytes 40
  7.2 15.7 %copy-start.5 = (f32[2,128]{1,0:T(2,128)S(1)}, f32[2,128]{1,0:T(2,128)}, u32[]{:S(2)}) copy-start(f32[2,128]{1,0:T(2,128)} %param.16) | copy-start | bytes 3076
  7.2 15.7 %copy-start.6 = (f32[2,128]{1,0:T(2,128)S(1)}, f32[2,128]{1,0:T(2,128)}, u32[]{:S(2)}) copy-start(f32[2,128]{1,0:T(2,128)} %param.17) | copy-start | bytes 3076
  7.2 121.1 %all-reduce.10.cloned.1.call-start = ((), (), s32[]{:S(2)}) async-start(), calls=%async_computation.1 | async-start | bytes 1769472 | tf_op jit(solution)/shard_map/psum | solution.py:121
  9.2 63.4 %collective-permute-start.8 = (bf16[2,32,1,8,128]{4,1,3,2,0:T(8,128)(2,1)S(1)}, bf16[2,32,1,8,128]{4,1,3,2,0:T(8,128)(2,1)S(1)}, u32[]{:S(2)}, u32[]{:S(2)}) collective-permute-start(bf16[2,32,1,8,128]{4,1,3,2,0:T(8,128)(2,1)S(1)} %get-tuple-element.41), channel_id=1, source_target_pairs={{0,4},{4,8},{8,12},{12,16},{16,20},{20,24},{24,28},{28,0},{1,5},{5... | collective-permute-start | bytes 393224 | tf_op jit(solution)/shard_map/ppermute | solution.py:14
  12.2 60.4 %collective-permute-start.9 = (bf16[2,32,1,8,128]{4,1,3,2,0:T(8,128)(2,1)S(1)}, bf16[2,32,1,8,128]{4,1,3,2,0:T(8,128)(2,1)S(1)}, u32[]{:S(2)}, u32[]{:S(2)}) collective-permute-start(bf16[2,32,1,8,128]{4,1,3,2,0:T(8,128)(2,1)S(1)} %get-tuple-element.42), channel_id=1, source_target_pairs={{4,0},{8,4},{12,8},{16,12},{20,16},{24,20},{28,24},{0,28},{5,1},{9... | collective-permute-start | bytes 393224 | tf_op jit(solution)/shard_map/ppermute | solution.py:17
  23.3 7.0 %collective-permute-start = (bf16[32,1,8,128]{3,0,2,1:T(8,128)(2,1)S(1)}, bf16[32,1,8,128]{3,0,2,1:T(8,128)(2,1)S(1)}, u32[]{:S(2)}, u32[]{:S(2)}) collective-permute-start(bf16[32,1,8,128]{3,0,2,1:T(8,128)(2,1)S(1)} %get-tuple-element.53), channel_id=1, source_target_pairs={{0,4},{4,8},{8,12},{12,16},{16,20},{20,24},{24,28},{28,0},{1,5},{5... | collective-permute-start | bytes 196616 | tf_op jit(solution)/shard_map/ppermute | solution.py:14
  23.4 7.0 %collective-permute-start.1 = (bf16[32,1,8,128]{3,0,2,1:T(8,128)(2,1)S(1)}, bf16[32,1,8,128]{3,0,2,1:T(8,128)(2,1)S(1)}, u32[]{:S(2)}, u32[]{:S(2)}) collective-permute-start(bf16[32,1,8,128]{3,0,2,1:T(8,128)(2,1)S(1)} %get-tuple-element.54), channel_id=1, source_target_pairs={{4,0},{8,4},{12,8},{16,12},{20,16},{24,20},{28,24},{0,28},{5,1},{9... | collective-permute-start | bytes 196616 | tf_op jit(solution)/shard_map/ppermute | solution.py:17
  30.4 29.8 %collective-permute-start.2 = (bf16[32,4,1,128]{3,0,2,1:T(8,128)(2,1)S(1)}, bf16[32,4,1,128]{3,0,2,1:T(8,128)(2,1)S(1)}, u32[]{:S(2)}, u32[]{:S(2)}) collective-permute-start(bf16[32,4,1,128]{3,0,2,1:T(8,128)(2,1)S(1)} %get-tuple-element.49), channel_id=1, source_target_pairs={{0,1},{1,2},{2,3},{3,0},{4,5},{5,6},{6,7},{7,4},{8,9},{9,10},{10,1... | collective-permute-start | bytes 98312 | tf_op jit(solution)/shard_map/ppermute | solution.py:14
  30.4 29.8 %collective-permute-start.3 = (bf16[32,4,1,128]{3,0,2,1:T(8,128)(2,1)S(1)}, bf16[32,4,1,128]{3,0,2,1:T(8,128)(2,1)S(1)}, u32[]{:S(2)}, u32[]{:S(2)}) collective-permute-start(bf16[32,4,1,128]{3,0,2,1:T(8,128)(2,1)S(1)} %get-tuple-element.50), channel_id=1, source_target_pairs={{1,0},{2,1},{3,2},{0,3},{5,4},{6,5},{7,6},{4,7},{9,8},{10,9},{11,1... | collective-permute-start | bytes 98312 | tf_op jit(solution)/shard_map/ppermute | solution.py:17
  60.4 0.9 copy-start.2
  66.7 0.9 copy-start.4
  67.8 7.0 %collective-permute-start.4 = (bf16[32,1,8,128]{3,0,2,1:T(8,128)(2,1)S(1)}, bf16[32,1,8,128]{3,0,2,1:T(8,128)(2,1)S(1)}, u32[]{:S(2)}, u32[]{:S(2)}) collective-permute-start(bf16[32,1,8,128]{3,0,2,1:T(8,128)(2,1)S(1)} %get-tuple-element.51), channel_id=1, source_target_pairs={{0,4},{4,8},{8,12},{12,16},{16,20},{20,24},{24,28},{28,0},{1,5},{5... | collective-permute-start | bytes 196616 | tf_op jit(solution)/shard_map/ppermute | solution.py:14
  67.9 7.0 %collective-permute-start.5 = (bf16[32,1,8,128]{3,0,2,1:T(8,128)(2,1)S(1)}, bf16[32,1,8,128]{3,0,2,1:T(8,128)(2,1)S(1)}, u32[]{:S(2)}, u32[]{:S(2)}) collective-permute-start(bf16[32,1,8,128]{3,0,2,1:T(8,128)(2,1)S(1)} %get-tuple-element.52), channel_id=1, source_target_pairs={{4,0},{8,4},{12,8},{16,12},{20,16},{24,20},{28,24},{0,28},{5,1},{9... | collective-permute-start | bytes 196616 | tf_op jit(solution)/shard_map/ppermute | solution.py:17
  72.6 4.0 %collective-permute-start.10 = (bf16[2,32,4,1,128]{4,1,3,2,0:T(8,128)(2,1)S(1)}, bf16[2,32,4,1,128]{4,1,3,2,0:T(8,128)(2,1)S(1)}, u32[]{:S(2)}, u32[]{:S(2)}) collective-permute-start(bf16[2,32,4,1,128]{4,1,3,2,0:T(8,128)(2,1)S(1)} %get-tuple-element.31), channel_id=1, source_target_pairs={{0,1},{1,2},{2,3},{3,0},{4,5},{5,6},{6,7},{7,4},{8,9},{9,10},{10,1... | collective-permute-start | bytes 196616 | tf_op jit(solution)/shard_map/ppermute | solution.py:14
  72.7 4.0 %collective-permute-start.11 = (bf16[2,32,4,1,128]{4,1,3,2,0:T(8,128)(2,1)S(1)}, bf16[2,32,4,1,128]{4,1,3,2,0:T(8,128)(2,1)S(1)}, u32[]{:S(2)}, u32[]{:S(2)}) collective-permute-start(bf16[2,32,4,1,128]{4,1,3,2,0:T(8,128)(2,1)S(1)} %get-tuple-element.32), channel_id=1, source_target_pairs={{1,0},{2,1},{3,2},{0,3},{5,4},{6,5},{7,6},{4,7},{9,8},{10,9},{11,1... | collective-permute-start | bytes 196616 | tf_op jit(solution)/shard_map/ppermute | solution.py:17
  74.9 17.2 %collective-permute-start.6 = (bf16[32,4,1,128]{3,0,2,1:T(8,128)(2,1)S(1)}, bf16[32,4,1,128]{3,0,2,1:T(8,128)(2,1)S(1)}, u32[]{:S(2)}, u32[]{:S(2)}) collective-permute-start(bf16[32,4,1,128]{3,0,2,1:T(8,128)(2,1)S(1)} %get-tuple-element.45), channel_id=1, source_target_pairs={{0,1},{1,2},{2,3},{3,0},{4,5},{5,6},{6,7},{7,4},{8,9},{9,10},{10,1... | collective-permute-start | bytes 98312 | tf_op jit(solution)/shard_map/ppermute | solution.py:14
  74.9 17.2 %collective-permute-start.7 = (bf16[32,4,1,128]{3,0,2,1:T(8,128)(2,1)S(1)}, bf16[32,4,1,128]{3,0,2,1:T(8,128)(2,1)S(1)}, u32[]{:S(2)}, u32[]{:S(2)}) collective-permute-start(bf16[32,4,1,128]{3,0,2,1:T(8,128)(2,1)S(1)} %get-tuple-element.46), channel_id=1, source_target_pairs={{1,0},{2,1},{3,2},{0,3},{5,4},{6,5},{7,6},{4,7},{9,8},{10,9},{11,1... | collective-permute-start | bytes 98312 | tf_op jit(solution)/shard_map/ppermute | solution.py:17
  91.9 116.2 %all-reduce.8.cloned.1.call-start = ((), (), s32[]{:S(2)}) async-start(), calls=%async_computation | async-start | bytes 1769472 | tf_op jit(solution)/shard_map/psum | solution.py:121
  92.4 0.9 copy-start.1
Sparse Core Ops, SparseCore 0:
  92.0 36.2 all-reduce.9
  131.7 76.2 all-reduce.7
